TPU v7x, 256 devices: a whole 4x4x8 slice. The times are simulated.
256 devices in a mesh: seg: 8 (over y, core), sec: 32 (over x, z).
Axes of the slice: x: 4, y: 4, z: 8, core: 2. Of those that a mesh axis runs over, the one named last changes fastest.
Arguments:
- psi_init: float32 [8, 32, 256, 256], P('seg', 'sec'), may hold values from -6 to 6
- boundary_env: float32 [32, 18, 256, 256], P('sec')
- right_env: float32 [8, 32, 18, 256, 256], P('seg', 'sec')
- transfer_blocks: float32 [8, 32, 256, 256], P('seg', 'sec')
- transfer_mix: float32 [8, 18, 18], P('seg')
- hop_left: float32 [8, 32, 256, 256], P('seg', 'sec'), may hold values from -0.75 to 0.75
- hop_right: float32 [8, 32, 256, 256], P('seg', 'sec'), may hold values from -0.75 to 0.75
- block_sizes: int32 [8, 2, 32], P('seg'), may hold values from 64 to 256, as said below
- sources: int32 [8, 32], P('seg'), may hold values from 0 to 31, each once within a row
Outputs:
- state: float32 [8, 32, 256, 256], P('seg', 'sec')
Inputs may be any that keep to these rules, and one draw needn't show every extreme that they name: `sources`: each block number appears once in a segment's list. `block_sizes`: each segment has a block with 256 live rows and one with 256 live columns.
All inputs are finite; a program needn't handle non-finite values.
Results may differ from a plain program's by a relative error of at most 0.0003.
Values sent between devices are 32-bit elements; how exact they have to be, the bound alone decides.
No kernel may reach another device: no remote copies, remote signals or barrier semaphores. Data moves between devices by JAX's collectives and lax.ppermute only.
A program may use at most 128 MiB of HBM per device.

v0:
```python
import jax
import jax.numpy as jnp
from jax import lax
from jax.sharding import PartitionSpec as P

DAV = 2


HIGH = lax.Precision.HIGHEST
EPSILON = 1e-06


def passed_along(value, axis, steps):
    count = lax.axis_size(axis)
    initial, last = (max(0, -steps), min(count, count - steps))
    return lax.ppermute(value, axis, [(source, source + steps) for source in range(initial, last)])


def product(left, right):
    return jnp.matmul(left, right, precision=HIGH)


def combine(earlier, later):
    return (product(earlier[0], later[0]), product(earlier[1], later[1]))


def norm_total(vector):
    return lax.psum(jnp.sum(vector * vector), "sec")


def per_device(
    psi_init,
    boundary_env,
    right_env,
    transfer_blocks,
    transfer_mix,
    hop_left,
    hop_right,
    block_sizes,
    sources,
):
    initial = psi_init[0]
    right_side = right_env[0]
    own_blocks = transfer_blocks[0]
    own_mix = transfer_mix[0]
    left_hop = hop_left[0]
    right_hop = hop_right[0]
    all_sizes = block_sizes[0]
    all_sources = sources[0]
    local_blocks = initial.shape[0]
    block_width = initial.shape[1]
    channels = own_mix.shape[0]
    sector_count = lax.axis_size("sec")
    first_block = lax.axis_index("sec") * local_blocks
    eye_mix = jnp.eye(channels, dtype=jnp.float32)
    eye_blocks = jnp.broadcast_to(jnp.eye(block_width, dtype=jnp.float32), own_blocks.shape)
    prefix_mix, prefix_blocks = (eye_mix, eye_blocks)
    leading = lax.axis_index("seg") == 0
    for hop_index in range(lax.axis_size("seg") - 1):
        carry_mix, carry_blocks = combine((prefix_mix, prefix_blocks), (own_mix, own_blocks))
        got_mix, got_blocks = passed_along((carry_mix, carry_blocks), "seg", 1)
        prefix_mix = jnp.where(leading, eye_mix, got_mix)
        prefix_blocks = jnp.where(leading, eye_blocks, got_blocks)
    turned = product(
        product(jnp.swapaxes(prefix_blocks, 1, 2)[:, None], boundary_env), prefix_blocks[:, None]
    )
    left_env = jnp.einsum("vw,bvij->bwij", prefix_mix, turned, precision=HIGH)
    live_sizes = lax.dynamic_slice_in_dim(all_sizes, first_block, local_blocks, 1)
    wanted = lax.dynamic_slice_in_dim(all_sources, first_block, local_blocks, 0)
    places = lax.broadcasted_iota(jnp.int32, (1, block_width), 1)
    row_live = (places < live_sizes[0][:, None]).astype(jnp.float32)
    col_live = (places < live_sizes[1][:, None]).astype(jnp.float32)
    masking = row_live[:, :, None] * col_live[:, None, :]
    diagonal = jnp.einsum(
        "bwi,bwj->bij",
        jnp.diagonal(left_env, axis1=2, axis2=3),
        jnp.diagonal(right_side, axis1=2, axis2=3),
        precision=HIGH,
    )
    vector = masking * initial
    vector = vector / jnp.sqrt(norm_total(vector) + EPSILON)
    for turn_index in range(DAV):
        local_part = jnp.sum(product(product(left_env, vector[:, None]), right_side), axis=1)
        moving = product(vector, right_hop)
        shard_piece = lax.all_gather(moving, "sec", axis=0, tiled=True)
        global_ids = lax.broadcasted_iota(jnp.int32, (1, shard_piece.shape[0]), 1)
        chooser = (wanted[:, None] == global_ids).astype(jnp.float32)
        regrouped = jnp.zeros_like(moving) + jnp.einsum(
            "ji,ipc->jpc", chooser, shard_piece, precision=HIGH
        )
        image_vec = masking * (local_part + product(left_hop, regrouped))
        rayleigh = lax.psum(jnp.sum(vector * image_vec), "sec")
        residue = image_vec - rayleigh * vector
        shifted = diagonal - rayleigh
        update = vector - residue * shifted / (shifted * shifted + 1.0)
        vector = update / jnp.sqrt(norm_total(update) + EPSILON)
    cells = float(local_blocks * sector_count * block_width * block_width)
    return (vector * jnp.sqrt(jnp.float32(cells)))[None]


def solution(mesh):
    return jax.shard_map(
        per_device,
        mesh=mesh,
        in_specs=(
            P("seg", "sec", None, None),
            P("sec", None, None, None),
            P("seg", "sec", None, None, None),
            P("seg", "sec", None, None),
            P("seg", None, None),
            P("seg", "sec", None, None),
            P("seg", "sec", None, None),
            P("seg", None, None),
            P("seg", None),
        ),
        out_specs=P("seg", "sec", None, None),
        check_vma=False,
    )
```

profile of v0, /device:TPU:16, one launch (start us, length us, event | category | flops | bytes accessed | tf_op | source)
XLA Modules:
  0.0 646.7 jit_solution(14586238692061087781)
XLA Ops:
  10.8 78.3 %psum.35 = f32[]{:T(128)} all-reduce(f32[]{:T(128)} %fusion.65), channel_id=1, replica_groups=mesh['seg'=8,'sec'=32] {'sec'}, use_global_device_ids=true, to_apply=%region_1.2 | all-reduce | flops 1 | bytes 8 | tf_op jit(solution)/shard_map/psum | solution.py:28
  94.2 5.8 collective-permute-done
  102.3 5.8 collective-permute-done.1
  110.4 5.8 collective-permute-done.2
  119.3 3.3 collective-permute-start.7
  127.6 3.3 collective-permute-start.4
  133.0 3.1 collective-permute-done.9
  143.3 3.1 collective-permute-done.11
  152.1 18.1 %copy.26 = f32[1,1,18,256,256]{2,4,3,1,0:T(8,128)} copy(f32[1,1,18,256,256]{4,3,2,1,0:T(8,128)} %param.11) | data formatting | bytes 9437184 | tf_op args[2]
  174.8 6.1 fusion.12
  181.0 4.0 fusion.10
  185.0 10.1 %fusion.18 = f32[18,256,256]{2,0,1:T(8,128)} fusion(f32[18,256,256]{2,1,0:T(8,128)S(1)} %fusion.10, f32[18,18]{1,0:T(8,128)S(1)} %collective-permute-done.13, pred[]{:T(512)S(6)} %eq.62), kind=kOutput, calls=%fused_computation.20 | convolution fusion | flops 254804944 | bytes 9438481 | tf_op jit(solution)/shard_map/vw,bvij->bwij/dot_general | solution.py:67
  195.1 17.6 %copy.29 = f32[18,256,256]{0,2,1:T(8,128)} copy(f32[18,256,256]{2,0,1:T(8,128)} %fusion.18) | data formatting | bytes 9437184 | tf_op jit(solution)/shard_map/squeeze | solution.py:20
  215.1 7.9 %fusion.16 = f32[18,256,256]{2,1,0:T(8,128)S(1)} fusion(f32[18,256,256]{2,0,1:T(8,128)} %fusion.18, f32[1,1,256,256]{3,2,1,0:T(8,128)S(1)} %copy-done.2, f32[]{:T(128)S(6)} %sqrt.9, f32[256]{0:T(256)S(1)} %get-tuple-element.16, f32[256]{0:T(256)S(1)} %get-tuple-element.17), kind=kOutput, calls=%fused_computation.18 | convolution fusion | flops 3624075264 | bytes 9701380 | tf_op jit(solution)/shard_map/dot_general | solution.py:20
  223.0 9.9 %fusion.28 = f32[256,256]{1,0:T(8,128)S(1)} fusion(f32[18,256,256]{2,1,0:T(8,128)S(1)} %fusion.16, f32[1,1,18,256,256]{4,3,2,1,0:T(8,128)} %param.11), kind=kOutput, calls=%fused_computation.35 | convolution fusion | flops 3623878656 | bytes 9699328 | tf_op jit(solution)/shard_map/dot_general | solution.py:20
  232.9 11.0 %fusion.2 = f32[1,256,256]{2,0,1:T(1,128)S(1)} fusion(f32[32,256,256]{2,1,0:T(8,128)} %bitcast.185, s32[]{:T(128)} %bitcast.34), kind=kOutput, calls=%fused_computation.4 | convolution fusion | flops 25165856 | bytes 8650756 | tf_op jit(solution)/shard_map/ji,ipc->jpc/dot_general | solution.py:88
  245.0 70.2 %psum.36 = f32[]{:T(128)} all-reduce(f32[]{:T(128)} %get-tuple-element.11), channel_id=1, replica_groups=mesh['seg'=8,'sec'=32] {'sec'}, use_global_device_ids=true, to_apply=%region_3.4 | all-reduce | flops 1 | bytes 8 | tf_op jit(solution)/shard_map/psum | solution.py:92
  317.0 72.1 %psum.37 = f32[]{:T(128)} all-reduce(f32[]{:T(128)} %get-tuple-element.7), channel_id=1, replica_groups=mesh['seg'=8,'sec'=32] {'sec'}, use_global_device_ids=true, to_apply=%region_5.6 | all-reduce | flops 1 | bytes 8 | tf_op jit(solution)/shard_map/psum | solution.py:28
  390.9 7.8 %fusion.14 = f32[18,256,256]{2,1,0:T(8,128)S(1)} fusion(f32[18,256,256]{2,0,1:T(8,128)} %fusion.18, f32[256,256]{1,0:T(8,128)S(1)} %get-tuple-element.8, f32[]{:T(128)S(6)} %sqrt.10), kind=kOutput, calls=%fused_computation.16 | convolution fusion | flops 3623944192 | bytes 9699332 | tf_op jit(solution)/shard_map/dot_general | solution.py:20
  398.8 4.1 fusion.25
  402.8 79.7 %all-gather.7.cloned.1.call-done = f32[8192,256]{1,0:T(8,128)} async-done(((f32[256,256]{1,0:T(8,128)}), f32[8192,256]{1,0:T(8,128)}) %all-gather.7.cloned.1.call-update) | async-done | bytes 8388624 | tf_op jit(solution)/shard_map/all_gather | solution.py:85
  482.6 11.0 %fusion = f32[1,256,256]{2,0,1:T(1,128)S(1)} fusion(f32[32,256,256]{2,1,0:T(8,128)} %bitcast.186, s32[]{:T(128)} %bitcast.34), kind=kOutput, calls=%fused_computation.2 | convolution fusion | flops 25165856 | bytes 8650756 | tf_op jit(solution)/shard_map/ji,ipc->jpc/dot_general | solution.py:88
  494.6 71.9 %psum.38 = f32[]{:T(128)} all-reduce(f32[]{:T(128)} %get-tuple-element.14), channel_id=1, replica_groups=mesh['seg'=8,'sec'=32] {'sec'}, use_global_device_ids=true, to_apply=%region_7.8 | all-reduce | flops 1 | bytes 8 | tf_op jit(solution)/shard_map/psum | solution.py:92
  567.8 70.5 %psum.39 = f32[]{:T(128)} all-reduce(f32[]{:T(128)} %get-tuple-element.5), channel_id=1, replica_groups=mesh['seg'=8,'sec'=32] {'sec'}, use_global_device_ids=true, to_apply=%region_9.10 | all-reduce | flops 1 | bytes 8 | tf_op jit(solution)/shard_map/psum | solution.py:28
  (74 shorter events, 50.2 us)
Async XLA Ops:
  6.5 85.4 %copy-start = (f32[1,1,256,256]{3,2,1,0:T(8,128)S(1)}, f32[1,1,256,256]{3,2,1,0:T(8,128)}, u32[]{:S(2)}) copy-start(f32[1,1,256,256]{3,2,1,0:T(8,128)} %param.12) | copy-start | bytes 786436
  6.5 124.3 %copy-start.3 = (f32[1,18,18]{2,0,1:T(1,128)S(1)}, f32[1,18,18]{2,0,1:T(1,128)}, u32[]{:S(2)}) copy-start(f32[1,18,18]{2,0,1:T(1,128)} %param.13) | copy-start | bytes 3892
  6.5 145.0 %copy-start.6 = (s32[1,32]{1,0:T(1,128)S(1)}, s32[1,32]{1,0:T(1,128)}, u32[]{:S(2)}) copy-start(s32[1,32]{1,0:T(1,128)} %param.17) | copy-start | bytes 388
  6.5 226.4 %all-gather.5.cloned.1.call-start = ((), (), s32[]{:S(2)}) async-start(), calls=%async_computation | async-start | bytes 8650752 | tf_op jit(solution)/shard_map/all_gather | solution.py:85
  91.9 390.6 %all-gather.7.cloned.1.call-start = ((), (), s32[]{:S(2)}) async-start(), calls=%async_computation.1 | async-start | bytes 8650752 | tf_op jit(solution)/shard_map/all_gather | solution.py:85
  92.3 7.7 %collective-permute-start = (f32[1,256,256]{2,1,0:T(8,128)S(1)}, f32[1,256,256]{2,1,0:T(8,128)S(1)}, u32[]{:S(2)}, u32[]{:S(2)}) collective-permute-start(f32[1,256,256]{2,1,0:T(8,128)S(1)} %convolution_bitcast_fusion.8), channel_id=1, source_target_pairs={{0,32},{32,64},{64,96},{96,128},{128,160},{160,192},{192,224},{1,3... | collective-permute-start | bytes 786440 | tf_op jit(solution)/shard_map/ppermute | solution.py:16
  100.4 7.7 %collective-permute-start.1 = (f32[1,256,256]{2,1,0:T(8,128)S(1)}, f32[1,256,256]{2,1,0:T(8,128)S(1)}, u32[]{:S(2)}, u32[]{:S(2)}) collective-permute-start(f32[1,256,256]{2,1,0:T(8,128)S(1)} %convolution_bitcast_fusion.7), channel_id=1, source_target_pairs={{0,32},{32,64},{64,96},{96,128},{128,160},{160,192},{192,224},{1,3... | collective-permute-start | bytes 786440 | tf_op jit(solution)/shard_map/ppermute | solution.py:16
  108.5 7.7 %collective-permute-start.2 = (f32[1,256,256]{2,1,0:T(8,128)S(1)}, f32[1,256,256]{2,1,0:T(8,128)S(1)}, u32[]{:S(2)}, u32[]{:S(2)}) collective-permute-start(f32[1,256,256]{2,1,0:T(8,128)S(1)} %convolution_bitcast_fusion.6), channel_id=1, source_target_pairs={{0,32},{32,64},{64,96},{96,128},{128,160},{160,192},{192,224},{1,3... | collective-permute-start | bytes 786440 | tf_op jit(solution)/shard_map/ppermute | solution.py:16
  116.6 10.6 %collective-permute-start.3 = (f32[1,256,256]{2,1,0:T(8,128)S(1)}, f32[1,256,256]{2,1,0:T(8,128)S(1)}, u32[]{:S(2)}, u32[]{:S(2)}) collective-permute-start(f32[1,256,256]{2,1,0:T(8,128)S(1)} %convolution_bitcast_fusion.5), channel_id=1, source_target_pairs={{0,32},{32,64},{64,96},{96,128},{128,160},{160,192},{192,224},{1,3... | collective-permute-start | bytes 786440 | tf_op jit(solution)/shard_map/ppermute | solution.py:16
  119.3 5.1 collective-permute-start.7
  125.2 5.7 collective-permute-start.8
  127.6 10.6 %collective-permute-start.4 = (f32[1,256,256]{2,1,0:T(8,128)S(1)}, f32[1,256,256]{2,1,0:T(8,128)S(1)}, u32[]{:S(2)}, u32[]{:S(2)}) collective-permute-start(f32[1,256,256]{2,1,0:T(8,128)S(1)} %convolution_bitcast_fusion.4), channel_id=1, source_target_pairs={{0,32},{32,64},{64,96},{96,128},{128,160},{160,192},{192,224},{1,3... | collective-permute-start | bytes 786440 | tf_op jit(solution)/shard_map/ppermute | solution.py:16
  131.0 5.0 collective-permute-start.9
  136.2 5.0 collective-permute-start.10
  138.5 9.9 %collective-permute-start.5 = (f32[1,256,256]{2,1,0:T(8,128)S(1)}, f32[1,256,256]{2,1,0:T(8,128)S(1)}, u32[]{:S(2)}, u32[]{:S(2)}) collective-permute-start(f32[1,256,256]{2,1,0:T(8,128)S(1)} %convolution_bitcast_fusion.3), channel_id=1, source_target_pairs={{0,32},{32,64},{64,96},{96,128},{128,160},{160,192},{192,224},{1,3... | collective-permute-start | bytes 786440 | tf_op jit(solution)/shard_map/ppermute | solution.py:16
  141.4 5.0 collective-permute-start.11
  146.5 26.0 %collective-permute-start.12 = (f32[18,18]{1,0:T(8,128)S(1)}, f32[18,18]{1,0:T(8,128)S(1)}, u32[]{:S(2)}, u32[]{:S(2)}) collective-permute-start(f32[18,18]{1,0:T(8,128)S(1)} %fusion.80), channel_id=1, source_target_pairs={{0,32},{32,64},{64,96},{96,128},{128,160},{160,192},{192,224},{1,3... | collective-permute-start | bytes 3896 | tf_op jit(solution)/shard_map/ppermute | solution.py:16
  148.9 26.0 %collective-permute-start.6 = (f32[1,256,256]{2,1,0:T(8,128)S(1)}, f32[1,256,256]{2,1,0:T(8,128)S(1)}, u32[]{:S(2)}, u32[]{:S(2)}) collective-permute-start(f32[1,256,256]{2,1,0:T(8,128)S(1)} %convolution_bitcast_fusion.2), channel_id=1, source_target_pairs={{0,32},{32,64},{64,96},{96,128},{128,160},{160,192},{192,224},{1,3... | collective-permute-start | bytes 786440 | tf_op jit(solution)/shard_map/ppermute | solution.py:16
  172.7 12.3 %collective-permute-start.13 = (f32[18,18]{1,0:T(8,128)S(1)}, f32[18,18]{1,0:T(8,128)S(1)}, u32[]{:S(2)}, u32[]{:S(2)}) collective-permute-start(f32[18,18]{1,0:T(8,128)S(1)} %fusion.81), channel_id=1, source_target_pairs={{0,32},{32,64},{64,96},{96,128},{128,160},{160,192},{192,224},{1,3... | collective-permute-start | bytes 3896 | tf_op jit(solution)/shard_map/ppermute | solution.py:16
  195.1 20.0 %copy-start.2 = (f32[1,1,256,256]{3,2,1,0:T(8,128)S(1)}, f32[1,1,256,256]{3,2,1,0:T(8,128)}, u32[]{:S(2)}) copy-start(f32[1,1,256,256]{3,2,1,0:T(8,128)} %param.9) | copy-start | bytes 786436
  232.9 11.1 %copy-start.5 = (f32[1,1,256,256]{3,2,1,0:T(8,128)S(1)}, f32[1,1,256,256]{3,2,1,0:T(8,128)}, u32[]{:S(2)}) copy-start(f32[1,1,256,256]{3,2,1,0:T(8,128)} %param.14) | copy-start | bytes 786436
  232.9 156.9 %copy-start.4 = (f32[1,1,256,256]{3,2,1,0:T(8,128)S(1)}, f32[1,1,256,256]{3,2,1,0:T(8,128)}, u32[]{:S(2)}) copy-start(f32[1,1,256,256]{3,2,1,0:T(8,128)} %param.15) | copy-start | bytes 786436
  315.2 83.5 %slice-start = ((s8[4718592]{0:T(1024)(128)(4,1)}), s8[524288]{0:T(1024)(128)(4,1)S(1)}, s32[]{:S(2)}) async-start(s8[4718592]{0:T(1024)(128)(4,1)} %bitcast.182), calls=%async_computation.2 | async-start | bytes 1048576
  482.6 157.2 %copy-start.1 = (f32[1,1,256,256]{3,2,1,0:T(8,128)S(1)}, f32[1,1,256,256]{3,2,1,0:T(8,128)}, u32[]{:S(2)}) copy-start(f32[1,1,256,256]{3,2,1,0:T(8,128)} %param.12) | copy-start | bytes 786436
  (1 other events, 7.8 us)
Sparse Core Ops, SparseCore 0:
  92.1 91.4 all-gather.4
  391.0 91.4 all-gather.6
where the time goes:
time: 653 us; the launch traced here: 647 us
  blocking collectives  363 us (56%)
  waiting for transfers between devices  105 us (16%)
  matrix products  84 us (13%)
  local copies, waits for them, and re-layouts  42.3 us (6%)
  starting transfers between devices  31.3 us (5%)
  between operations  16.1 us (2%)
    psum x3, blocking collectives, norm_total(): return lax.psum(jnp.sum(vector * vector), 'sec')  221 us
    psum x2, blocking collectives, per_device(): rayleigh = lax.psum(jnp.sum(vector * image_vec), 'sec')  142 us
    all_gather x2, waiting for transfers between devices, per_device(): shard_piece = lax.all_gather(moving, 'sec', axis=0, tiled=True)  79.7 us
    dot_general x24, matrix products, product(): return jnp.matmul(left, right, precision=HIGH)  50 us
    ppermute x14, starting transfers between devices, passed_along(): lax.ppermute(value, axis, [(source, source + steps) for source in range(i...  31.3 us
    ppermute x14, waiting for transfers between devices, passed_along(): lax.ppermute(value, axis, [(source, source + steps) for source in range(i...  25.3 us
    dot_general x2, matrix products, per_device(): jnp.einsum('ji,ipc->jpc', chooser, shard_piece, precision=HIGH)  22 us
    unnamed x19, local copies, waits for them, and re-layouts  18.1 us
  transfers between devices with their start and end apart: 16, of which 7 were waited for; matrix products, arithmetic and copies ran while one was open for 15% of the time, Pallas kernels for 0%

commit v1 on v0

v1 whole, which is shorter than its diff:
```python
import jax
import jax.numpy as jnp
from jax import lax
from jax.sharding import PartitionSpec as P

DAV = 2


HIGH = lax.Precision.HIGHEST
EPSILON = 1e-06


def passed_along(value, axis, steps):
    count = lax.axis_size(axis)
    initial, last = (max(0, -steps), min(count, count - steps))
    return lax.ppermute(value, axis, [(source, source + steps) for source in range(initial, last)])


def product(left, right):
    return jnp.matmul(left, right, precision=HIGH)


def sec_total(values):
    count = lax.axis_size("sec")
    spread = jnp.broadcast_to(values[None, :], (count, values.shape[0]))
    return jnp.sum(lax.all_to_all(spread, "sec", 0, 0, tiled=True), axis=0)


def regroup(moving, wanted):
    count = lax.axis_size("sec")
    rows, cols = moving.shape
    pieces = moving.reshape(count, rows // count, cols)
    held = lax.all_to_all(pieces, "sec", 0, 0, tiled=True)
    ordered = jnp.take(held, wanted, axis=0, mode="clip")
    back = lax.all_to_all(ordered, "sec", 0, 0, tiled=True)
    return back.reshape(rows, cols)


def prefix_scan(own_mix, own_blocks):
    seg = lax.axis_index("seg")
    count = lax.axis_size("seg")
    width = own_blocks.shape[0]
    channels = own_mix.shape[0]
    pad = -(-channels // 8) * 8
    eye_mix = jnp.eye(channels, dtype=jnp.float32)
    eye_blocks = jnp.eye(width, dtype=jnp.float32)
    span_mix, span_blocks = own_mix, own_blocks
    before_mix, before_blocks = eye_mix, eye_blocks
    step = 1
    while step < count:
        packed = jnp.concatenate(
            [span_blocks, jnp.pad(span_mix, ((0, pad - channels), (0, width - channels)))], axis=0
        )
        got = passed_along(packed, "seg", step)
        got_blocks = got[:width]
        got_mix = got[width:width + channels, :channels]
        take = seg >= step
        if step == 1:
            before_mix = jnp.where(take, got_mix, eye_mix)
            before_blocks = jnp.where(take, got_blocks, eye_blocks)
        else:
            before_mix = jnp.where(take, product(got_mix, before_mix), before_mix)
            before_blocks = jnp.where(take, product(got_blocks, before_blocks), before_blocks)
        if step * 2 < count:
            span_mix = jnp.where(take, product(got_mix, span_mix), span_mix)
            span_blocks = jnp.where(take, product(got_blocks, span_blocks), span_blocks)
        step *= 2
    return before_mix, before_blocks


def per_device(
    psi_init,
    boundary_env,
    right_env,
    transfer_blocks,
    transfer_mix,
    hop_left,
    hop_right,
    block_sizes,
    sources,
):
    initial = psi_init[0, 0]
    boundary = boundary_env[0]
    right_side = right_env[0, 0]
    own_blocks = transfer_blocks[0, 0]
    own_mix = transfer_mix[0]
    left_hop = hop_left[0, 0]
    right_hop = hop_right[0, 0]
    all_sizes = block_sizes[0]
    all_sources = sources[0]
    block_width = initial.shape[1]
    sector_count = lax.axis_size("sec")
    me = lax.axis_index("sec")

    places = lax.broadcasted_iota(jnp.int32, (block_width,), 0)
    row_live = (places < all_sizes[0, me]).astype(jnp.float32)
    col_live = (places < all_sizes[1, me]).astype(jnp.float32)
    masking = row_live[:, None] * col_live[None, :]

    first = masking * initial
    first_moved = regroup(product(first, right_hop), all_sources)

    prefix_mix, prefix_blocks = prefix_scan(own_mix, own_blocks)
    half = jnp.einsum("ukl,lj->ukj", boundary, prefix_blocks, precision=HIGH)
    turned = jnp.einsum("ki,ukj->uij", prefix_blocks, half, precision=HIGH)
    left_env = jnp.einsum("uw,uij->wij", prefix_mix, turned, precision=HIGH)
    diagonal = jnp.einsum(
        "wi,wj->ij",
        jnp.diagonal(left_env, axis1=1, axis2=2),
        jnp.diagonal(right_side, axis1=1, axis2=2),
        precision=HIGH,
    )

    def apply_h(vector, moved):
        inner = jnp.einsum("wij,jk->wik", left_env, vector, precision=HIGH)
        local_part = jnp.einsum("wik,wkl->il", inner, right_side, precision=HIGH)
        return masking * (local_part + product(left_hop, moved))

    def step(vector, image_vec, rayleigh):
        residue = image_vec - rayleigh * vector
        shifted = diagonal - rayleigh
        return vector - residue * shifted / (shifted * shifted + 1.0)

    image = apply_h(first, first_moved)
    sums = sec_total(jnp.stack([jnp.sum(first * first), jnp.sum(first * image)]))
    scale = 1.0 / jnp.sqrt(sums[0] + EPSILON)
    vector = first * scale
    image_vec = image * scale
    rayleigh = sums[1] / (sums[0] + EPSILON)
    for turn_index in range(1, DAV):
        update = step(vector, image_vec, rayleigh)
        moved = regroup(product(update, right_hop), all_sources)
        image = apply_h(update, moved)
        sums = sec_total(jnp.stack([jnp.sum(update * update), jnp.sum(update * image)]))
        scale = 1.0 / jnp.sqrt(sums[0] + EPSILON)
        vector = update * scale
        image_vec = image * scale
        rayleigh = sums[1] / (sums[0] + EPSILON)
    update = step(vector, image_vec, rayleigh)
    total = sec_total(jnp.sum(update * update)[None])[0]
    cells = float(sector_count * block_width * block_width)
    return (update * (jnp.sqrt(jnp.float32(cells)) / jnp.sqrt(total + EPSILON)))[None, None]


def solution(mesh):
    return jax.shard_map(
        per_device,
        mesh=mesh,
        in_specs=(
            P("seg", "sec", None, None),
            P("sec", None, None, None),
            P("seg", "sec", None, None, None),
            P("seg", "sec", None, None),
            P("seg", None, None),
            P("seg", "sec", None, None),
            P("seg", "sec", None, None),
            P("seg", None, None),
            P("seg", None),
        ),
        out_specs=P("seg", "sec", None, None),
        check_vma=False,
    )
```

time: 653 us -> 232 us (0.36)
  blocking collectives: 363 us -> 53.4 us
  waiting for transfers between devices: 105 us -> 16.1 us
  matrix products: 84 us -> 52.5 us
  local copies, waits for them, and re-layouts: 42.3 us -> 56.6 us
  between operations: 16.1 us -> 4.18 us
    psum x5 -> x0, blocking collectives: 363 us -> none  [the longest x3 221 us: norm_total(): return lax.psum(jnp.sum(vector * vector), 'sec')]
    all_gather x2 -> x0, waiting for transfers between devices: 79.7 us -> none  [per_device(): shard_piece = lax.all_gather(moving, 'sec', axis=0, tiled=True)]
    all_to_all x0 -> x3, blocking collectives: none -> 53.4 us  [the longest x2 32.2 us: sec_total(): return jnp.sum(lax.all_to_all(spread, 'sec', 0, 0, tiled=True), axis=0)]
    dot_general x24 -> x12, matrix products: 50 us -> 8.44 us  [product(): return jnp.matmul(left, right, precision=HIGH)]
    all_to_all x0 -> x4, starting transfers between devices: none -> 30.8 us  [the longest x1 11.3 us: regroup(): held = lax.all_to_all(pieces, 'sec', 0, 0, tiled=True)]
    ppermute x14 -> x3, starting transfers between devices: 31.3 us -> 6.58 us  [passed_along(): lax.ppermute(value, axis, [(source, source + steps) for source in range(i...]
    dot_general x0 -> x1, local copies, waits for them, and re-layouts: none -> 17.6 us  [per_device(): left_env = jnp.einsum('uw,uij->wij', prefix_mix, turned, precision=HIGH)]
    squeeze x1 -> x0, local copies, waits for them, and re-layouts: 17.6 us -> none  [product(): return jnp.matmul(left, right, precision=HIGH)]
  transfers between devices with their start and end apart: 16 -> 7, of which waited for: 7 -> 2; matrix products, arithmetic and copies ran while one was open for 15% -> 44% of each run, Pallas kernels for 0% -> 0%
where the time goes in v1:
time: 232 us; the launch traced here: 228 us
  local copies, waits for them, and re-layouts  56.6 us (24%)
  blocking collectives  53.4 us (23%)
  matrix products  52.5 us (23%)
  starting transfers between devices  37.3 us (16%)
  waiting for transfers between devices  16.1 us (7%)
  other arithmetic  7.7 us (3%)
  between operations  4.18 us (2%)
    all_to_all x2, blocking collectives, sec_total(): return jnp.sum(lax.all_to_all(spread, 'sec', 0, 0, tiled=True), axis=0)  32.2 us
    unnamed x18, local copies, waits for them, and re-layouts  21.5 us
    all_to_all x1, blocking collectives, regroup(): held = lax.all_to_all(pieces, 'sec', 0, 0, tiled=True)  21.2 us
    dot_general x1, local copies, waits for them, and re-layouts, per_device(): left_env = jnp.einsum('uw,uij->wij', prefix_mix, turned, precision=HIGH)  17.6 us
    dot_general x2, matrix products, apply_h(): inner = jnp.einsum('wij,jk->wik', left_env, vector, precision=HIGH)  12.5 us
    all_to_all x1, starting transfers between devices, regroup(): held = lax.all_to_all(pieces, 'sec', 0, 0, tiled=True)  11.3 us
    ppermute x3, waiting for transfers between devices, passed_along(): lax.ppermute(value, axis, [(source, source + steps) for source in range(i...  9.93 us
    all_to_all x1, starting transfers between devices, sec_total(): return jnp.sum(lax.all_to_all(spread, 'sec', 0, 0, tiled=True), axis=0)  9.75 us
  transfers between devices with their start and end apart: 7, of which 2 were waited for; matrix products, arithmetic and copies ran while one was open for 44% of the time, Pallas kernels for 0%

profile of v1, /device:TPU:16, one launch (start us, length us, event | category | flops | bytes accessed | tf_op | source)
XLA Modules:
  0.0 227.7 jit_solution(14375327256618086815)
XLA Ops:
  6.2 2.2 fusion.31
  8.4 11.3 %all-to-all-start = ((f32[32,8,256]{2,1,0:T(8,128)}), f32[32,8,256]{2,1,0:T(8,128)S(1)}, u32[]{:S(2)}, u32[]{:S(2)}) async-start(f32[32,8,256]{2,1,0:T(8,128)} %fusion.31), calls=%async_computation | async-start | bytes 524288 | tf_op jit(solution)/shard_map/all_to_all | solution.py:33
  22.1 3.2 %collective-permute-start.1 = (f32[280,256]{1,0:T(8,128)S(1)}, f32[280,256]{1,0:T(8,128)S(1)}, u32[]{:S(2)}, u32[]{:S(2)}) collective-permute-start(f32[280,256]{1,0:T(8,128)S(1)} %select_maximum_fusion.1), channel_id=1, source_target_pairs={{0,64},{32,96},{64,128},{96,160},{128,192},{160,224},{1,65},{33,97... | collective-permute-start | bytes 860168 | tf_op jit(solution)/shard_map/ppermute | solution.py:16
  25.9 6.1 %all-to-all-done = f32[32,8,256]{2,1,0:T(8,128)S(1)} async-done(((f32[32,8,256]{2,1,0:T(8,128)}), f32[32,8,256]{2,1,0:T(8,128)S(1)}, u32[]{:S(2)}, u32[]{:S(2)}) %all-to-all-start) | async-done | bytes 262176 | tf_op jit(solution)/shard_map/all_to_all | solution.py:33
  33.4 5.8 %all-to-all-start.1 = ((f32[32,8,256]{2,1,0:T(8,128)}), f32[32,8,256]{2,1,0:T(8,128)S(1)}, u32[]{:S(2)}, u32[]{:S(2)}) async-start(f32[32,8,256]{2,1,0:T(8,128)} %gather_fusion), calls=%async_computation.1 | async-start | bytes 524288 | tf_op jit(solution)/shard_map/all_to_all | solution.py:35
  41.8 9.9 %collective-permute-done.2 = f32[280,256]{1,0:T(8,128)S(1)} collective-permute-done((f32[280,256]{1,0:T(8,128)S(1)}, f32[280,256]{1,0:T(8,128)S(1)}, u32[]{:S(2)}, u32[]{:S(2)}) %collective-permute-start.2) | collective-permute-done | bytes 286752 | tf_op jit(solution)/shard_map/ppermute | solution.py:16
  52.1 9.7 %fusion.6 = f32[256,18,256]{2,0,1:T(8,128)S(1)} fusion(f32[256,256,1]{1,0,2:T(8,128)S(1)} %fusion.15, f32[1,18,256,256]{3,2,1,0:T(8,128)} %param.10), kind=kOutput, calls=%fused_computation.10 | convolution fusion | flops 3623878656 | bytes 9699328 | tf_op jit(solution)/shard_map/ukl,lj->ukj/dot_general | solution.py:104
  61.8 5.5 %fusion.12 = f32[18,256,256]{1,2,0:T(8,128)} fusion(f32[256,256,1]{1,0,2:T(8,128)S(1)} %fusion.15, f32[256,18,256]{2,0,1:T(8,128)S(1)} %fusion.6), kind=kOutput, calls=%fused_computation.16 | convolution fusion | flops 3623878656 | bytes 9699328 | tf_op jit(solution)/shard_map/ki,ukj->uij/dot_general | solution.py:105
  67.3 6.4 %copy.34 = f32[18,256,256]{2,0,1:T(8,128)} copy(f32[18,256,256]{1,2,0:T(8,128)} %fusion.12) | data formatting | bytes 9437184 | tf_op jit(solution)/shard_map/ki,ukj->uij/transpose | solution.py:105
  73.8 7.8 %fusion.64 = f32[18,256,256]{2,0,1:T(8,128)S(1)} fusion(f32[18,18,1]{1,0,2:T(8,128)S(1)} %fusion.26, f32[18,256,256]{2,0,1:T(8,128)} %copy.34), kind=kOutput, calls=%fused_computation.96 | convolution fusion | flops 254803968 | bytes 9438480 | tf_op jit(solution)/shard_map/uw,uij->wij/dot_general | solution.py:106
  81.6 2.6 %copy-done.1 = f32[18,256,256]{2,0,1:T(8,128)} copy-done((f32[18,256,256]{2,0,1:T(8,128)}, f32[18,256,256]{2,0,1:T(8,128)S(1)}, u32[]{:S(2)}) %copy-start.1) | copy-done | bytes 4718616
  84.2 4.8 %fusion.10 = f32[18,256,256]{2,1,0:T(8,128)S(1)} fusion(f32[18,256,256]{2,0,1:T(8,128)S(1)} %fusion.64, f32[1,1,256,256]{3,2,1,0:T(8,128)S(1)} %copy-done.2, f32[256]{0:T(256)S(1)} %get-tuple-element.21, f32[256]{0:T(256)S(1)} %get-tuple-element.22), kind=kOutput, calls=%fused_computation.14 | convolution fusion | flops 3624009728 | bytes 9701376 | tf_op jit(solution)/shard_map/wij,jk->wik/dot_general | solution.py:115
  89.1 4.0 %fusion.23 = f32[256,256]{1,0:T(8,128)S(1)} fusion(f32[18,256,256]{2,1,0:T(8,128)S(1)} %fusion.10, f32[1,1,18,256,256]{4,3,2,1,0:T(8,128)S(1)} %bitcast.130), kind=kOutput, calls=%fused_computation.29 | convolution fusion | flops 3623878656 | bytes 9699328 | tf_op jit(solution)/shard_map/wik,wkl->il/dot_general | solution.py:116
  96.0 9.7 %all-to-all-start.2 = ((f32[32,1,2]{2,1,0:T(1,128)}), f32[32,1,2]{2,1,0:T(1,128)S(1)}, u32[]{:S(2)}, u32[]{:S(2)}) async-start(f32[32,1,2]{2,1,0:T(1,128)} %broadcast_in_dim.34), calls=%async_computation.2 | async-start | bytes 32768 | tf_op jit(solution)/shard_map/all_to_all | solution.py:26
  105.8 18.1 %copy.36 = f32[1,1,18,256,256]{2,4,3,1,0:T(8,128)} copy(f32[1,1,18,256,256]{4,3,2,1,0:T(8,128)} %param.11) | data formatting | bytes 9437184 | tf_op args[2]
  123.9 2.3 %gather_fusion.2 = f32[256,18]{1,0:T(8,128)S(1)} fusion(f32[18,256,256]{0,2,1:T(8,128)} %bitcast.133, s32[256]{0:T(256)S(1)} %bitcast.127), kind=kCustom, calls=%fused_computation.2 | custom fusion | bytes 38912 | tf_op jit(solution)/shard_map/jit(diagonal)/gather | solution.py:110
  126.3 17.6 %copy.39 = f32[18,256,256]{0,2,1:T(8,128)} copy(f32[18,256,256]{2,0,1:T(8,128)} %copy-done.1) | data formatting | bytes 9437184 | tf_op jit(solution)/shard_map/uw,uij->wij/dot_general | solution.py:106
  143.9 2.3 %gather_fusion.1 = f32[256,18]{1,0:T(8,128)S(1)} fusion(f32[18,256,256]{0,2,1:T(8,128)} %copy.39, s32[256]{0:T(256)S(1)} %bitcast.128), kind=kCustom, calls=%fused_computation.1 | custom fusion | bytes 38912 | tf_op jit(solution)/shard_map/jit(diagonal)/gather | solution.py:109
  149.0 21.2 %all_to_all.38 = f32[32,8,256]{2,1,0:T(8,128)S(1)} all-to-all(f32[32,8,256]{2,1,0:T(8,128)S(1)} %fusion.29), channel_id=1, replica_groups=mesh['seg'=8,'sec'=32] {'sec'}, dimensions={0} | all-to-all | bytes 524288 | tf_op jit(solution)/shard_map/all_to_all | solution.py:33
  171.5 3.9 %all-to-all-start.4 = ((f32[32,8,256]{2,1,0:T(8,128)}), f32[32,8,256]{2,1,0:T(8,128)S(1)}, u32[]{:S(2)}, u32[]{:S(2)}) async-start(f32[32,8,256]{2,1,0:T(8,128)} %gather_fusion.3), calls=%async_computation.4 | async-start | bytes 524288 | tf_op jit(solution)/shard_map/all_to_all | solution.py:35
  175.4 7.7 %fusion.8 = f32[18,256,256]{2,1,0:T(8,128)S(1)} fusion(f32[18,256,256]{2,0,1:T(8,128)} %copy-done.1, f32[256,256]{1,0:T(8,128)S(1)} %get-tuple-element.18), kind=kOutput, calls=%fused_computation.12 | convolution fusion | flops 3623878656 | bytes 9699328 | tf_op jit(solution)/shard_map/wij,jk->wik/dot_general | solution.py:115
  183.1 4.1 %fusion.20 = f32[256,256]{1,0:T(8,128)S(1)} fusion(f32[18,256,256]{2,1,0:T(8,128)S(1)} %fusion.8, f32[1,1,18,256,256]{4,3,2,1,0:T(8,128)S(1)} %bitcast.132), kind=kOutput, calls=%fused_computation.28 | convolution fusion | flops 3623878656 | bytes 9699328 | tf_op jit(solution)/shard_map/wik,wkl->il/dot_general | solution.py:116
  189.5 19.4 %all_to_all.39 = f32[32,1,2]{2,1,0:T(1,128)S(1)} all-to-all(f32[32,1,2]{2,1,0:T(1,128)S(1)} %broadcast_in_dim.35), channel_id=1, replica_groups=mesh['seg'=8,'sec'=32] {'sec'}, dimensions={0} | all-to-all | bytes 512 | tf_op jit(solution)/shard_map/all_to_all | solution.py:26
  212.5 12.8 %all_to_all.40 = f32[32,1,1]{2,1,0:T(1,128)S(1)} all-to-all(f32[32,1,1]{2,1,0:T(1,128)S(1)} %broadcast_in_dim.36), channel_id=1, replica_groups=mesh['seg'=8,'sec'=32] {'sec'}, dimensions={0} | all-to-all | bytes 256 | tf_op jit(solution)/shard_map/all_to_all | solution.py:26
  (58 shorter events, 25.1 us)
Async XLA Ops:
  0.0 93.1 %copy-start = (f32[1,1,256,256]{3,2,1,0:T(8,128)S(1)}, f32[1,1,256,256]{3,2,1,0:T(8,128)}, u32[]{:S(2)}) copy-start(f32[1,1,256,256]{3,2,1,0:T(8,128)} %param.14) | copy-start | bytes 786436
  1.7 18.0 %collective-permute-start = (f32[280,256]{1,0:T(8,128)S(1)}, f32[280,256]{1,0:T(8,128)S(1)}, u32[]{:S(2)}, u32[]{:S(2)}) collective-permute-start(f32[280,256]{1,0:T(8,128)S(1)} %select_maximum_fusion.2), channel_id=1, source_target_pairs={{0,32},{32,64},{64,96},{96,128},{128,160},{160,192},{192,224},{1,3... | collective-permute-start | bytes 860168 | tf_op jit(solution)/shard_map/ppermute | solution.py:16
  8.4 23.7 %all-to-all-start = ((f32[32,8,256]{2,1,0:T(8,128)}), f32[32,8,256]{2,1,0:T(8,128)S(1)}, u32[]{:S(2)}, u32[]{:S(2)}) async-start(f32[32,8,256]{2,1,0:T(8,128)} %fusion.31), calls=%async_computation | async-start | bytes 524288 | tf_op jit(solution)/shard_map/all_to_all | solution.py:33
  22.1 17.1 %collective-permute-start.1 = (f32[280,256]{1,0:T(8,128)S(1)}, f32[280,256]{1,0:T(8,128)S(1)}, u32[]{:S(2)}, u32[]{:S(2)}) collective-permute-start(f32[280,256]{1,0:T(8,128)S(1)} %select_maximum_fusion.1), channel_id=1, source_target_pairs={{0,64},{32,96},{64,128},{96,160},{128,192},{160,224},{1,65},{33,97... | collective-permute-start | bytes 860168 | tf_op jit(solution)/shard_map/ppermute | solution.py:16
  33.4 59.8 %all-to-all-start.1 = ((f32[32,8,256]{2,1,0:T(8,128)}), f32[32,8,256]{2,1,0:T(8,128)S(1)}, u32[]{:S(2)}, u32[]{:S(2)}) async-start(f32[32,8,256]{2,1,0:T(8,128)} %gather_fusion), calls=%async_computation.1 | async-start | bytes 524288 | tf_op jit(solution)/shard_map/all_to_all | solution.py:35
  39.7 12.0 %collective-permute-start.2 = (f32[280,256]{1,0:T(8,128)S(1)}, f32[280,256]{1,0:T(8,128)S(1)}, u32[]{:S(2)}, u32[]{:S(2)}) collective-permute-start(f32[280,256]{1,0:T(8,128)S(1)} %select_maximum_fusion), channel_id=1, source_target_pairs={{0,128},{32,160},{64,192},{96,224},{1,129},{33,161},{65,193},{97,2... | collective-permute-start | bytes 860168 | tf_op jit(solution)/shard_map/ppermute | solution.py:16
  67.3 21.8 %slice-start = ((s8[4718592]{0:T(1024)(128)(4,1)}), s8[524288]{0:T(1024)(128)(4,1)S(1)}, s32[]{:S(2)}) async-start(s8[4718592]{0:T(1024)(128)(4,1)} %bitcast.129), calls=%async_computation.7 | async-start | bytes 1048576
  73.8 10.4 %copy-start.2 = (f32[1,1,256,256]{3,2,1,0:T(8,128)S(1)}, f32[1,1,256,256]{3,2,1,0:T(8,128)}, u32[]{:S(2)}) copy-start(f32[1,1,256,256]{3,2,1,0:T(8,128)} %param.9) | copy-start | bytes 786436
  73.8 15.3 %slice-start.1 = ((s8[4718592]{0:T(1024)(128)(4,1)}), s8[4194304]{0:T(1024)(128)(4,1)S(1)}, s32[]{:S(2)}) async-start(s8[4718592]{0:T(1024)(128)(4,1)} %bitcast.129), calls=%async_computation.8 | async-start | bytes 8388608
  81.6 2.6 %copy-start.1 = (f32[18,256,256]{2,0,1:T(8,128)}, f32[18,256,256]{2,0,1:T(8,128)S(1)}, u32[]{:S(2)}) copy-start(f32[18,256,256]{2,0,1:T(8,128)S(1)} %fusion.64) | copy-start | bytes 14155780
  96.0 50.2 %all-to-all-start.2 = ((f32[32,1,2]{2,1,0:T(1,128)}), f32[32,1,2]{2,1,0:T(1,128)S(1)}, u32[]{:S(2)}, u32[]{:S(2)}) async-start(f32[32,1,2]{2,1,0:T(1,128)} %broadcast_in_dim.34), calls=%async_computation.2 | async-start | bytes 32768 | tf_op jit(solution)/shard_map/all_to_all | solution.py:26
  126.3 22.3 %copy-start.3 = (f32[1,1,256,256]{3,2,1,0:T(8,128)S(1)}, f32[1,1,256,256]{3,2,1,0:T(8,128)}, u32[]{:S(2)}) copy-start(f32[1,1,256,256]{3,2,1,0:T(8,128)} %param.15) | copy-start | bytes 786436
  148.6 34.5 %slice-start.2 = ((s8[4718592]{0:T(1024)(128)(4,1)}), s8[524288]{0:T(1024)(128)(4,1)S(1)}, s32[]{:S(2)}) async-start(s8[4718592]{0:T(1024)(128)(4,1)} %bitcast.131), calls=%async_computation.9 | async-start | bytes 1048576
  171.5 15.7 %all-to-all-start.4 = ((f32[32,8,256]{2,1,0:T(8,128)}), f32[32,8,256]{2,1,0:T(8,128)S(1)}, u32[]{:S(2)}, u32[]{:S(2)}) async-start(f32[32,8,256]{2,1,0:T(8,128)} %gather_fusion.3), calls=%async_computation.4 | async-start | bytes 524288 | tf_op jit(solution)/shard_map/all_to_all | solution.py:35
  175.4 7.7 %slice-start.3 = ((s8[4718592]{0:T(1024)(128)(4,1)}), s8[4194304]{0:T(1024)(128)(4,1)S(1)}, s32[]{:S(2)}) async-start(s8[4718592]{0:T(1024)(128)(4,1)} %bitcast.131), calls=%async_computation.10 | async-start | bytes 8388608
